TPU v7x, 512 devices: a whole 4x8x8 slice. The times are simulated.
512 devices in a mesh: segment: 8 (over z), gy: 64 (over x, y, core).
Axes of the slice: x: 4, y: 8, z: 8, core: 2. Of those that a mesh axis runs over, the one named last changes fastest.
Arguments:
- acts: bfloat16 [8, 8, 128, 32, 256], P('segment', None, 'gy'), may hold values from -6 to 6
- grad_out: bfloat16 [8, 128, 32, 256], P('segment', 'gy'), may hold values from -6 to 6
- w_plane: bfloat16 [8, 3, 3, 32, 32], P('segment'), may hold values from -0.375 to 0.375
- w_depth: bfloat16 [8, 3, 32, 32], P('segment'), may hold values from -0.625 to 0.625
- tiles: int32 [64, 12], P('gy'), may hold values from -1 to 15, as said below
Outputs:
- grad_in: bfloat16 [8, 128, 32, 256], P('segment', 'gy')
- grad_plane: float32 [8, 3, 3, 32, 32], P('segment')
- grad_depth: float32 [8, 3, 32, 32], P('segment')
Inputs may be any that keep to these rules, and one draw needn't show every extreme that they name: Row s lists distinct tiles z * 2 + x-tile of slab s in its first entries and -1 after them; each row lists 1 to 12 tiles, and some row lists exactly 12.
All inputs are finite; a program needn't handle non-finite values.
Results may differ from a plain program's by a relative error of at most 0.02.
Values may be sent and summed in bfloat16 or wider, within the bound.
No kernel may reach another device: no remote copies, remote signals or barrier semaphores. Data moves between devices by JAX's collectives and lax.ppermute only.
A program may use at most 64 MiB of HBM per device.

v0:
```python
import math
import jax
import jax.numpy as jnp
from jax import lax
from jax.sharding import PartitionSpec as P

TILE = 128


def padded_2(block, sides, width):
    for axis, dim in sides:
        count = lax.axis_size(axis)
        forward = [(i, i + 1) for i in range(count - 1)]
        backward = [(target, source) for source, target in forward]
        low = lax.ppermute(
            lax.slice_in_dim(block, block.shape[dim] - width, None, axis=dim), axis, forward
        )
        high = lax.ppermute(lax.slice_in_dim(block, 0, width, axis=dim), axis, backward)
        block = jnp.concatenate([low, block, high], axis=dim)
    return block


def width_pad(field):
    return jnp.pad(field, [(0, 0)] * (field.ndim - 1) + [(1, 1)])


def plane_conv_all(rows_in, kernel, height, width):
    padded = width_pad(rows_in)
    total = None
    for i in range(3):
        for j in range(3):
            term = jnp.einsum(
                "loc,lzycx->lzyox",
                kernel[:, i, j],
                padded[:, :, i : i + height, :, j : j + width],
                preferred_element_type=jnp.float32,
            )
            total = term if total is None else total + term
    return total


def depth_conv_all(deep, kernel, depth):
    total = None
    for k in range(3):
        term = jnp.einsum(
            "loc,lzycx->lzyox",
            kernel[:, k],
            deep[:, k : k + depth],
            preferred_element_type=jnp.float32,
        )
        total = term if total is None else total + term
    return total


def plane_back(rows_grad, kernel, height, width):
    padded = width_pad(rows_grad)
    total = None
    for i in range(3):
        for j in range(3):
            term = jnp.einsum(
                "oc,...yox->...ycx",
                kernel[i, j],
                padded[..., 2 - i : 2 - i + height, :, 2 - j : 2 - j + width],
                preferred_element_type=jnp.float32,
            )
            total = term if total is None else total + term
    return total


def plane_taps(grad_mid, rows_in, height, width):
    padded = width_pad(rows_in)
    rows_out = []
    for i in range(3):
        row_taps = []
        for j in range(3):
            row_taps.append(
                jnp.einsum(
                    "...yox,...ycx->oc",
                    grad_mid,
                    padded[..., i : i + height, :, j : j + width],
                    preferred_element_type=jnp.float32,
                )
            )
        rows_out.append(jnp.stack(row_taps))
    return jnp.stack(rows_out)


def depth_back(mix_deep, kernel, depth):
    total = None
    for k in range(3):
        term = jnp.einsum(
            "oc,zyox->zycx",
            kernel[k],
            mix_deep[2 - k : 2 - k + depth],
            preferred_element_type=jnp.float32,
        )
        total = term if total is None else total + term
    return total


def depth_taps(grad_mix, deep, depth):
    return jnp.stack(
        [
            jnp.einsum(
                "zyox,zycx->oc", grad_mix, deep[k : k + depth], preferred_element_type=jnp.float32
            )
            for k in range(3)
        ]
    )


def silu_slope(value):
    sig = jax.nn.sigmoid(value)
    return sig * (1.0 + value * (1.0 - sig))


def local(acts, grad_out, w_plane, w_depth, tiles):
    sections = acts.shape[1]
    height = acts.shape[2]
    width = acts.shape[4]
    chans = w_plane.shape[3]
    count = lax.axis_size("segment")
    layers = count * acts.shape[0]
    zs = grad_out.shape[0]
    scale = 1.0 / math.sqrt(sections * height * lax.axis_size("gy") * width)
    segment = lax.axis_index("segment")
    mine = lax.all_to_all(acts, "segment", 1, 0, tiled=True)
    plane_w = lax.all_gather(w_plane, "segment", axis=0, tiled=True)
    depth_w = lax.all_gather(w_depth, "segment", axis=0, tiled=True)
    ids = (segment * zs + jnp.arange(zs, dtype=jnp.int32))[:, None] * (width // TILE) + jnp.arange(
        width // TILE, dtype=jnp.int32
    )[None, :]
    hit = jnp.any(tiles[0][None, None, :] == ids[:, :, None], axis=2)
    mask_full = jnp.repeat(hit.astype(jnp.float32), TILE, axis=1)[:, None, None, :]
    rows_own = padded_2(mine, (("gy", 2),), 1)
    mid = plane_conv_all(rows_own, plane_w, height, width).astype(jnp.bfloat16)
    deep = padded_2(mid, (("segment", 1),), 1)
    value = depth_conv_all(deep, depth_w, zs)
    factor = silu_slope(value) * mask_full[None]
    grad = grad_out
    plane_list = [None] * layers
    depth_list = [None] * layers
    for layer in reversed(range(layers)):
        grad_mix = (grad.astype(jnp.float32) * factor[layer]).astype(jnp.bfloat16)
        mix_deep = padded_2(grad_mix, (("segment", 0),), 1)
        grad_mid = depth_back(mix_deep, depth_w[layer], zs).astype(jnp.bfloat16)
        rows_grad = padded_2(grad_mid, (("gy", 1),), 1)
        grad = (
            grad.astype(jnp.float32) + plane_back(rows_grad, plane_w[layer], height, width)
        ).astype(jnp.bfloat16)
        depth_list[layer] = depth_taps(grad_mix, deep[layer], zs)
        plane_list[layer] = plane_taps(grad_mid, rows_own[layer], height, width)
    planes = jnp.stack(plane_list).reshape(layers, -1)
    depths = jnp.stack(depth_list).reshape(layers, -1)
    flat = jnp.concatenate([planes, depths], axis=1) * scale
    flat = lax.psum_scatter(flat, "segment", scatter_dimension=0, tiled=True)
    flat = lax.psum(flat, "gy")
    cut = planes.shape[1]
    plane_sum = flat[:, :cut].reshape(-1, 3, 3, chans, chans)
    depth_sum = flat[:, cut:].reshape(-1, 3, chans, chans)
    return (grad, plane_sum, depth_sum)


def solution(mesh):
    placed = (
        P("segment", None, "gy", None, None),
        P("segment", "gy", None, None),
        P("segment", None, None, None, None),
        P("segment", None, None, None),
        P("gy", None),
    )
    return jax.shard_map(
        local,
        mesh=mesh,
        in_specs=placed,
        out_specs=(
            P("segment", "gy", None, None),
            P("segment", None, None, None, None),
            P("segment", None, None, None),
        ),
        check_vma=False,
    )
```

profile of v0, /device:TPU:64, one launch (start us, length us, event | category | flops | bytes accessed | tf_op | source)
XLA Modules:
  0.0 603.1 jit_solution(2332710889217415071)
XLA Ops:
  7.2 10.0 %all-to-all-start = ((bf16[1,8,2,32,256]{4,3,2,0,1:T(8,128)(2,1)}), bf16[1,8,2,32,256]{4,3,2,0,1:T(8,128)(2,1)S(1)}, u32[]{:S(2)}, u32[]{:S(2)}) async-start(bf16[1,8,2,32,256]{4,3,2,0,1:T(8,128)(2,1)} %bitcast.2011), calls=%async_computation | async-start | bytes 524288 | tf_op jit(solution)/shard_map/all_to_all | solution.py:127
  17.4 1.3 dynamic-slice
  18.7 26.2 %all_gather.7 = bf16[8,3,32,32]{3,2,0,1:T(8,128)(2,1)S(1)} all-gather(bf16[1,3,32,32]{3,2,0,1:T(8,128)(2,1)S(1)} %bitcast.2013), channel_id=1, replica_groups=mesh['segment'=8,'gy'=64] {'segment'}, dimensions={0}, use_global_device_ids=true | all-gather | bytes 55296 | tf_op jit(solution)/shard_map/all_gather | solution.py:129
  44.9 25.8 %all_gather.6 = bf16[8,3,3,32,32]{4,3,0,2,1:T(8,128)(2,1)S(1)} all-gather(bf16[1,3,3,32,32]{4,3,0,2,1:T(8,128)(2,1)S(1)} %bitcast.2012), channel_id=1, replica_groups=mesh['segment'=8,'gy'=64] {'segment'}, dimensions={0}, use_global_device_ids=true | all-gather | bytes 165888 | tf_op jit(solution)/shard_map/all_gather | solution.py:128
  70.7 1.3 collective-permute-start
  72.0 1.3 collective-permute-start.1
  73.4 3.7 collective-permute-done.1
  79.5 1.9 collective-permute-start.3
  81.4 3.9 collective-permute-start.2
  85.6 2.3 collective-permute-done.3
  88.2 1.7 collective-permute-done.2
  90.4 4.2 collective-permute-start.5
  94.6 1.9 collective-permute-start.4
  97.3 3.2 collective-permute-done.4
  102.3 3.2 collective-permute-start.6
  105.5 1.3 collective-permute-start.7
  107.0 5.1 collective-permute-done.7
  114.2 5.6 collective-permute-start.9
  119.7 1.9 collective-permute-start.8
  122.3 4.4 collective-permute-done.8
  128.6 3.2 collective-permute-start.10
  131.8 1.3 collective-permute-start.11
  133.3 2.3 collective-permute-done.11
  137.7 3.9 collective-permute-start.13
  141.6 1.9 collective-permute-start.12
  144.2 3.2 collective-permute-done.12
  149.2 3.0 collective-permute-start.14
  152.2 1.3 collective-permute-start.15
  153.7 2.5 collective-permute-done.15
  158.3 3.1 collective-permute-start.17
  161.5 2.7 collective-permute-start.16
  164.9 2.4 collective-permute-done.16
  169.1 3.0 collective-permute-start.18
  172.1 1.3 collective-permute-start.19
  173.6 2.5 collective-permute-done.19
  178.2 3.1 collective-permute-start.21
  181.3 2.7 collective-permute-start.20
  184.8 2.4 collective-permute-done.20
  189.0 3.0 collective-permute-start.22
  192.0 1.3 collective-permute-start.23
  193.5 2.7 collective-permute-done.23
  198.3 3.1 collective-permute-start.25
  201.4 2.7 collective-permute-start.24
  204.8 2.4 collective-permute-done.24
  209.0 3.0 collective-permute-start.26
  212.0 1.3 collective-permute-start.27
  213.5 3.8 collective-permute-done.27
  219.3 3.1 collective-permute-start.29
  222.5 2.7 collective-permute-start.28
  225.9 2.4 collective-permute-done.28
  230.1 3.0 collective-permute-start.30
  233.1 1.3 collective-permute-start.31
  234.6 3.8 collective-permute-done.31
  240.4 3.1 collective-permute-start.33
  243.6 2.7 collective-permute-start.32
  247.1 2.2 collective-permute-done.32
  251.4 3.0 collective-permute-start.34
  254.4 1.3 collective-permute-start.35
  256.2 0.8 maximum_multiply_fusion
  257.0 2.6 collective-permute-done.35
  261.3 0.8 fusion.36
  262.1 84.7 %all-reduce.20.cloned.1.call-done = f32[8,12288]{1,0:T(8,128)} async-done(((f32[8,12288]{1,0:T(8,128)}), f32[8,12288]{1,0:T(8,128)}) %all-reduce.20.cloned.1.call-update) | async-done | bytes 393232
  346.9 1.7 constant_dynamic-slice_fusion
  348.5 246.2 %psum.7 = f32[1,12288]{1,0:T(1,128)S(1)} all-reduce(f32[1,12288]{1,0:T(1,128)S(1)} %constant_dynamic-slice_fusion), channel_id=1, replica_groups=mesh['segment'=8,'gy'=64] {'gy'}, use_global_device_ids=true, to_apply=%region_2.3 | all-reduce | flops 12288 | bytes 98304 | tf_op jit(solution)/shard_map/psum | solution.py:157
  (310 shorter events, 43.4 us)
Async XLA Ops:
  7.2 10.0 %copy-start.3 = (s32[1,12]{1,0:T(1,128)S(1)}, s32[1,12]{1,0:T(1,128)}, u32[]{:S(2)}) copy-start(s32[1,12]{1,0:T(1,128)} %param.9) | copy-start | bytes 148
  7.2 63.5 %all-to-all-start = ((bf16[1,8,2,32,256]{4,3,2,0,1:T(8,128)(2,1)}), bf16[1,8,2,32,256]{4,3,2,0,1:T(8,128)(2,1)S(1)}, u32[]{:S(2)}, u32[]{:S(2)}) async-start(bf16[1,8,2,32,256]{4,3,2,0,1:T(8,128)(2,1)} %bitcast.2011), calls=%async_computation | async-start | bytes 524288 | tf_op jit(solution)/shard_map/all_to_all | solution.py:127
  17.2 1.5 copy-start.2
  17.2 329.7 %all-reduce.20.cloned.1.call-start = ((), (), s32[]{:S(2)}) async-start(), calls=%async_computation.1 | async-start | bytes 786432
  18.6 26.2 %copy-start.1 = (bf16[1,3,3,32,32]{4,3,2,1,0:T(8,128)(2,1)S(1)}, bf16[1,3,3,32,32]{4,3,2,1,0:T(8,128)(2,1)}, u32[]{:S(2)}) copy-start(bf16[1,3,3,32,32]{4,3,2,1,0:T(8,128)(2,1)} %param.7) | copy-start | bytes 55300
  70.7 2.7 collective-permute-start
  72.0 5.0 collective-permute-start.1
  79.5 8.4 %collective-permute-start.3 = (bf16[8,1,2,32,256]{4,3,2,0,1:T(8,128)(2,1)S(1)}, bf16[8,1,2,32,256]{4,3,2,0,1:T(8,128)(2,1)S(1)}, u32[]{:S(2)}, u32[]{:S(2)}) collective-permute-start(bf16[8,1,2,32,256]{4,3,2,0,1:T(8,128)(2,1)S(1)} %bitcast.1994), channel_id=1, source_target_pairs={{64,0},{128,64},{192,128},{256,192},{320,256},{384,320},{448,384},... | collective-permute-start | bytes 786440 | tf_op jit(solution)/shard_map/ppermute | solution.py:18
  81.4 8.4 %collective-permute-start.2 = (bf16[8,1,2,32,256]{4,3,2,0,1:T(8,128)(2,1)S(1)}, bf16[8,1,2,32,256]{4,3,2,0,1:T(8,128)(2,1)S(1)}, u32[]{:S(2)}, u32[]{:S(2)}) collective-permute-start(bf16[8,1,2,32,256]{4,3,2,0,1:T(8,128)(2,1)S(1)} %bitcast.1995), channel_id=1, source_target_pairs={{0,64},{64,128},{128,192},{192,256},{256,320},{320,384},{384,448},... | collective-permute-start | bytes 786440 | tf_op jit(solution)/shard_map/ppermute | solution.py:15
  88.1 2.1 copy-start
  90.4 6.6 %collective-permute-start.5 = (bf16[1,2,32,256]{3,2,1,0:T(8,128)(2,1)S(1)}, bf16[1,2,32,256]{3,2,1,0:T(8,128)(2,1)S(1)}, u32[]{:S(2)}, u32[]{:S(2)}) collective-permute-start(bf16[1,2,32,256]{3,2,1,0:T(8,128)(2,1)S(1)} %fusion.86), channel_id=1, source_target_pairs={{0,64},{64,128},{128,192},{192,256},{256,320},{320,384},{384,448},... | collective-permute-start | bytes 98312 | tf_op jit(solution)/shard_map/ppermute | solution.py:15
  94.6 5.8 collective-permute-start.4
  102.3 4.7 collective-permute-start.6
  105.5 6.6 %collective-permute-start.7 = (bf16[1,1,32,256]{3,2,1,0:T(8,128)(2,1)S(1)}, bf16[1,1,32,256]{3,2,1,0:T(8,128)(2,1)S(1)}, u32[]{:S(2)}, u32[]{:S(2)}) collective-permute-start(bf16[1,1,32,256]{3,2,1,0:T(8,128)(2,1)S(1)} %get-tuple-element.36), channel_id=1, source_target_pairs={{1,0},{2,1},{3,2},{4,3},{5,4},{6,5},{7,6},{8,7},{9,8},{10,9},{11,1... | collective-permute-start | bytes 49160 | tf_op jit(solution)/shard_map/ppermute | solution.py:18
  114.2 8.0 %collective-permute-start.9 = (bf16[1,2,32,256]{3,2,1,0:T(8,128)(2,1)S(1)}, bf16[1,2,32,256]{3,2,1,0:T(8,128)(2,1)S(1)}, u32[]{:S(2)}, u32[]{:S(2)}) collective-permute-start(bf16[1,2,32,256]{3,2,1,0:T(8,128)(2,1)S(1)} %get-tuple-element.37), channel_id=1, source_target_pairs={{0,64},{64,128},{128,192},{192,256},{256,320},{320,384},{384,448},... | collective-permute-start | bytes 98312 | tf_op jit(solution)/shard_map/ppermute | solution.py:15
  119.7 7.0 %collective-permute-start.8 = (bf16[1,2,32,256]{3,2,1,0:T(8,128)(2,1)S(1)}, bf16[1,2,32,256]{3,2,1,0:T(8,128)(2,1)S(1)}, u32[]{:S(2)}, u32[]{:S(2)}) collective-permute-start(bf16[1,2,32,256]{3,2,1,0:T(8,128)(2,1)S(1)} %get-tuple-element.37), channel_id=1, source_target_pairs={{64,0},{128,64},{192,128},{256,192},{320,256},{384,320},{448,384},... | collective-permute-start | bytes 98312 | tf_op jit(solution)/shard_map/ppermute | solution.py:18
  128.6 4.7 collective-permute-start.10
  131.8 3.8 collective-permute-start.11
  137.7 6.4 %collective-permute-start.13 = (bf16[1,2,32,256]{3,2,1,0:T(8,128)(2,1)S(1)}, bf16[1,2,32,256]{3,2,1,0:T(8,128)(2,1)S(1)}, u32[]{:S(2)}, u32[]{:S(2)}) collective-permute-start(bf16[1,2,32,256]{3,2,1,0:T(8,128)(2,1)S(1)} %get-tuple-element.39), channel_id=1, source_target_pairs={{0,64},{64,128},{128,192},{192,256},{256,320},{320,384},{384,448},... | collective-permute-start | bytes 98312 | tf_op jit(solution)/shard_map/ppermute | solution.py:15
  141.6 5.8 collective-permute-start.12
  149.2 4.4 collective-permute-start.14
  152.2 4.0 collective-permute-start.15
  158.3 6.3 %collective-permute-start.17 = (bf16[1,2,32,256]{3,2,1,0:T(8,128)(2,1)S(1)}, bf16[1,2,32,256]{3,2,1,0:T(8,128)(2,1)S(1)}, u32[]{:S(2)}, u32[]{:S(2)}) collective-permute-start(bf16[1,2,32,256]{3,2,1,0:T(8,128)(2,1)S(1)} %get-tuple-element.41), channel_id=1, source_target_pairs={{0,64},{64,128},{128,192},{192,256},{256,320},{320,384},{384,448},... | collective-permute-start | bytes 98312 | tf_op jit(solution)/shard_map/ppermute | solution.py:15
  161.5 5.8 collective-permute-start.16
  169.1 4.4 collective-permute-start.18
  172.1 4.0 collective-permute-start.19
  178.2 6.3 %collective-permute-start.21 = (bf16[1,2,32,256]{3,2,1,0:T(8,128)(2,1)S(1)}, bf16[1,2,32,256]{3,2,1,0:T(8,128)(2,1)S(1)}, u32[]{:S(2)}, u32[]{:S(2)}) collective-permute-start(bf16[1,2,32,256]{3,2,1,0:T(8,128)(2,1)S(1)} %get-tuple-element.43), channel_id=1, source_target_pairs={{0,64},{64,128},{128,192},{192,256},{256,320},{320,384},{384,448},... | collective-permute-start | bytes 98312 | tf_op jit(solution)/shard_map/ppermute | solution.py:15
  181.3 5.8 collective-permute-start.20
  189.0 4.4 collective-permute-start.22
  192.0 4.2 collective-permute-start.23
  198.3 6.3 %collective-permute-start.25 = (bf16[1,2,32,256]{3,2,1,0:T(8,128)(2,1)S(1)}, bf16[1,2,32,256]{3,2,1,0:T(8,128)(2,1)S(1)}, u32[]{:S(2)}, u32[]{:S(2)}) collective-permute-start(bf16[1,2,32,256]{3,2,1,0:T(8,128)(2,1)S(1)} %get-tuple-element.45), channel_id=1, source_target_pairs={{0,64},{64,128},{128,192},{192,256},{256,320},{320,384},{384,448},... | collective-permute-start | bytes 98312 | tf_op jit(solution)/shard_map/ppermute | solution.py:15
  201.4 5.8 collective-permute-start.24
  209.0 4.4 collective-permute-start.26
  212.0 5.2 collective-permute-start.27
  219.3 6.3 %collective-permute-start.29 = (bf16[1,2,32,256]{3,2,1,0:T(8,128)(2,1)S(1)}, bf16[1,2,32,256]{3,2,1,0:T(8,128)(2,1)S(1)}, u32[]{:S(2)}, u32[]{:S(2)}) collective-permute-start(bf16[1,2,32,256]{3,2,1,0:T(8,128)(2,1)S(1)} %get-tuple-element.47), channel_id=1, source_target_pairs={{0,64},{64,128},{128,192},{192,256},{256,320},{320,384},{384,448},... | collective-permute-start | bytes 98312 | tf_op jit(solution)/shard_map/ppermute | solution.py:15
  222.5 5.8 collective-permute-start.28
  230.1 4.4 collective-permute-start.30
  233.1 5.2 collective-permute-start.31
  240.4 6.5 %collective-permute-start.33 = (bf16[1,2,32,256]{3,2,1,0:T(8,128)(2,1)S(1)}, bf16[1,2,32,256]{3,2,1,0:T(8,128)(2,1)S(1)}, u32[]{:S(2)}, u32[]{:S(2)}) collective-permute-start(bf16[1,2,32,256]{3,2,1,0:T(8,128)(2,1)S(1)} %get-tuple-element.49), channel_id=1, source_target_pairs={{0,64},{64,128},{128,192},{192,256},{256,320},{320,384},{384,448},... | collective-permute-start | bytes 98312 | tf_op jit(solution)/shard_map/ppermute | solution.py:15
  243.6 5.8 collective-permute-start.32
  251.4 5.6 collective-permute-start.34
  254.4 5.2 collective-permute-start.35
Sparse Core Ops, SparseCore 0:
  257.1 89.6 all-reduce.19
where the time goes:
time: 604 us; the launch traced here: 603 us
  blocking collectives  298 us (49%)
  waiting for transfers between devices  140 us (23%)
  starting transfers between devices  101 us (17%)
  matrix products  38.6 us (6%)
  between operations  15.3 us (3%)
  local copies, waits for them, and re-layouts  7.11 us (1%)
    psum x1, blocking collectives, local(): flat = lax.psum(flat, 'gy')  246 us
    unnamed x2, waiting for transfers between devices  84.7 us
    ppermute x18, starting transfers between devices, padded_2(): lax.ppermute(lax.slice_in_dim(block, block.shape[dim] - width, None, axis...  58.6 us
    ppermute x18, waiting for transfers between devices, padded_2(): lax.ppermute(lax.slice_in_dim(block, 0, width, axis=dim), axis, backward)  53.8 us
    ppermute x18, starting transfers between devices, padded_2(): lax.ppermute(lax.slice_in_dim(block, 0, width, axis=dim), axis, backward)  32.9 us
    all_gather x1, blocking collectives, local(): depth_w = lax.all_gather(w_depth, 'segment', axis=0, tiled=True)  26.2 us
    all_gather x1, blocking collectives, local(): plane_w = lax.all_gather(w_plane, 'segment', axis=0, tiled=True)  25.8 us
    dot_general x72, matrix products, plane_back(): jnp.einsum('oc,...yox->...ycx', kernel[i, j], padded[..., 2 - i:2 - i + h...  15 us
  transfers between devices with their start and end apart: 38, of which 20 were waited for; matrix products, arithmetic and copies ran while one was open for 2% of the time, Pallas kernels for 0%

commit v1 on v0

--- a/solution.py
+++ b/solution.py
@@ -154,7 +154,7 @@
     depths = jnp.stack(depth_list).reshape(layers, -1)
     flat = jnp.concatenate([planes, depths], axis=1) * scale
     flat = lax.psum_scatter(flat, "segment", scatter_dimension=0, tiled=True)
-    flat = lax.psum(flat, "gy")
+    flat = lax.all_gather(flat, "gy").sum(axis=0)
     cut = planes.shape[1]
     plane_sum = flat[:, :cut].reshape(-1, 3, 3, chans, chans)
     depth_sum = flat[:, cut:].reshape(-1, 3, chans, chans)

time: 604 us -> 444 us (0.74)
  the two profiles are of different devices: /device:TPU:64 before, /device:TPU:1 now
where the time goes in v1:
time: 444 us; the launch traced here: 443 us
  waiting for transfers between devices  209 us (47%)
  starting transfers between devices  123 us (28%)
  blocking collectives  41.8 us (9%)
  matrix products  38.6 us (9%)
  between operations  15.3 us (3%)
  local copies, waits for them, and re-layouts  7.72 us (2%)
  other arithmetic  7.44 us (2%)
    ppermute x18, starting transfers between devices, padded_2(): lax.ppermute(lax.slice_in_dim(block, block.shape[dim] - width, None, axis...  83.2 us
    unnamed x3, waiting for transfers between devices  81.4 us
    all_gather x1, waiting for transfers between devices, local(): flat = lax.all_gather(flat, 'gy').sum(axis=0)  72.8 us
    ppermute x18, waiting for transfers between devices, padded_2(): lax.ppermute(lax.slice_in_dim(block, 0, width, axis=dim), axis, backward)  53.1 us
    ppermute x18, starting transfers between devices, padded_2(): lax.ppermute(lax.slice_in_dim(block, 0, width, axis=dim), axis, backward)  28.9 us
    all_gather x1, blocking collectives, local(): depth_w = lax.all_gather(w_depth, 'segment', axis=0, tiled=True)  21.6 us
    all_gather x1, blocking collectives, local(): plane_w = lax.all_gather(w_plane, 'segment', axis=0, tiled=True)  20.2 us
    dot_general x72, matrix products, plane_back(): jnp.einsum('oc,...yox->...ycx', kernel[i, j], padded[..., 2 - i:2 - i + h...  15 us
  transfers between devices with their start and end apart: 39, of which 21 were waited for; matrix products, arithmetic and copies ran while one was open for 3% of the time, Pallas kernels for 0%

profile of v1, /device:TPU:1, one launch (start us, length us, event | category | flops | bytes accessed | tf_op | source)
XLA Modules:
  0.0 442.8 jit_solution(13929728282433312550)
XLA Ops:
  7.2 10.9 %all-to-all-start = ((bf16[1,8,2,32,256]{4,3,2,0,1:T(8,128)(2,1)}), bf16[1,8,2,32,256]{4,3,2,0,1:T(8,128)(2,1)S(1)}, u32[]{:S(2)}, u32[]{:S(2)}) async-start(bf16[1,8,2,32,256]{4,3,2,0,1:T(8,128)(2,1)} %bitcast.2014), calls=%async_computation | async-start | bytes 524288 | tf_op jit(solution)/shard_map/all_to_all | solution.py:127
  18.1 0.8 compare_reduce_fusion
  18.9 21.6 %all_gather.13 = bf16[8,3,32,32]{3,2,0,1:T(8,128)(2,1)S(1)} all-gather(bf16[1,3,32,32]{3,2,0,1:T(8,128)(2,1)} %bitcast.2018), channel_id=1, replica_groups=mesh['segment'=8,'gy'=64] {'segment'}, dimensions={0}, use_global_device_ids=true | all-gather | bytes 55296 | tf_op jit(solution)/shard_map/all_gather | solution.py:129
  40.6 20.2 %all_gather.12 = bf16[8,3,3,32,32]{4,3,0,2,1:T(8,128)(2,1)S(1)} all-gather(bf16[1,3,3,32,32]{4,3,0,2,1:T(8,128)(2,1)} %bitcast.2017), channel_id=1, replica_groups=mesh['segment'=8,'gy'=64] {'segment'}, dimensions={0}, use_global_device_ids=true | all-gather | bytes 165888 | tf_op jit(solution)/shard_map/all_gather | solution.py:128
  60.9 14.5 %collective-permute-start = (bf16[8,1,1,32,256]{4,3,2,0,1:T(8,128)(2,1)S(1)}, bf16[8,1,1,32,256]{4,3,2,0,1:T(8,128)(2,1)S(1)}, u32[]{:S(2)}, u32[]{:S(2)}) collective-permute-start(bf16[8,1,1,32,256]{4,3,2,0,1:T(8,128)(2,1)S(1)} %get-tuple-element.19), channel_id=1, source_target_pairs={{0,1},{1,2},{2,3},{3,4},{4,5},{5,6},{6,7},{7,8},{8,9},{9,10},{10,1... | collective-permute-start | bytes 393224 | tf_op jit(solution)/shard_map/ppermute | solution.py:15
  75.4 1.9 collective-permute-start.1
  77.4 4.3 collective-permute-done.1
  84.1 1.3 collective-permute-start.3
  85.4 4.8 %collective-permute-start.2 = (bf16[8,1,2,32,256]{4,3,2,0,1:T(8,128)(2,1)S(1)}, bf16[8,1,2,32,256]{4,3,2,0,1:T(8,128)(2,1)S(1)}, u32[]{:S(2)}, u32[]{:S(2)}) collective-permute-start(bf16[8,1,2,32,256]{4,3,2,0,1:T(8,128)(2,1)S(1)} %bitcast.1998), channel_id=1, source_target_pairs={{0,64},{64,128},{128,192},{192,256},{256,320},{320,384},{384,448},... | collective-permute-start | bytes 786440 | tf_op jit(solution)/shard_map/ppermute | solution.py:15
  90.5 1.6 collective-permute-done.3
  92.3 1.5 collective-permute-done.2
  94.3 3.8 collective-permute-start.5
  98.1 1.3 collective-permute-start.4
  100.1 2.9 collective-permute-done.4
  104.9 6.1 %collective-permute-start.6 = (bf16[1,1,32,256]{3,2,1,0:T(8,128)(2,1)S(1)}, bf16[1,1,32,256]{3,2,1,0:T(8,128)(2,1)S(1)}, u32[]{:S(2)}, u32[]{:S(2)}) collective-permute-start(bf16[1,1,32,256]{3,2,1,0:T(8,128)(2,1)S(1)} %get-tuple-element.35), channel_id=1, source_target_pairs={{0,1},{1,2},{2,3},{3,4},{4,5},{5,6},{6,7},{7,8},{8,9},{9,10},{10,1... | collective-permute-start | bytes 49160 | tf_op jit(solution)/shard_map/ppermute | solution.py:15
  111.1 1.9 collective-permute-start.7
  113.2 2.9 collective-permute-done.7
  118.2 3.6 collective-permute-start.9
  121.9 1.3 collective-permute-start.8
  123.9 4.6 %collective-permute-done.8 = bf16[1,2,32,256]{3,2,1,0:T(8,128)(2,1)S(1)} collective-permute-done((bf16[1,2,32,256]{3,2,1,0:T(8,128)(2,1)S(1)}, bf16[1,2,32,256]{3,2,1,0:T(8,128)(2,1)S(1)}, u32[]{:S(2)}, u32[]{:S(2)}) %collective-permute-start.8) | collective-permute-done | bytes 32800 | tf_op jit(solution)/shard_map/ppermute | solution.py:18
  130.3 3.1 collective-permute-start.10
  133.4 1.9 collective-permute-start.11
  135.5 2.9 collective-permute-done.11
  140.5 4.8 %collective-permute-start.13 = (bf16[1,2,32,256]{3,2,1,0:T(8,128)(2,1)S(1)}, bf16[1,2,32,256]{3,2,1,0:T(8,128)(2,1)S(1)}, u32[]{:S(2)}, u32[]{:S(2)}) collective-permute-start(bf16[1,2,32,256]{3,2,1,0:T(8,128)(2,1)S(1)} %get-tuple-element.39), channel_id=1, source_target_pairs={{0,64},{64,128},{128,192},{192,256},{256,320},{320,384},{384,448},... | collective-permute-start | bytes 98312 | tf_op jit(solution)/shard_map/ppermute | solution.py:15
  145.4 1.3 collective-permute-start.12
  147.4 2.9 collective-permute-done.12
  152.2 3.1 collective-permute-start.14
  155.3 1.9 collective-permute-start.15
  157.4 2.9 collective-permute-done.15
  162.4 3.6 collective-permute-start.17
  166.1 1.3 collective-permute-start.16
  168.1 2.7 collective-permute-done.16
  172.6 3.4 collective-permute-start.18
  175.9 1.9 collective-permute-start.19
  178.1 2.9 collective-permute-done.19
  183.1 2.8 collective-permute-start.21
  185.9 1.3 collective-permute-start.20
  187.9 2.7 collective-permute-done.20
  192.4 3.5 collective-permute-start.22
  196.0 1.9 collective-permute-start.23
  198.1 2.9 collective-permute-done.23
  203.1 2.8 collective-permute-start.25
  206.0 1.3 collective-permute-start.24
  208.0 2.7 collective-permute-done.24
  212.5 4.6 %collective-permute-start.26 = (bf16[1,1,32,256]{3,2,1,0:T(8,128)(2,1)S(1)}, bf16[1,1,32,256]{3,2,1,0:T(8,128)(2,1)S(1)}, u32[]{:S(2)}, u32[]{:S(2)}) collective-permute-start(bf16[1,1,32,256]{3,2,1,0:T(8,128)(2,1)S(1)} %get-tuple-element.25), channel_id=1, source_target_pairs={{0,1},{1,2},{2,3},{3,4},{4,5},{5,6},{6,7},{7,8},{8,9},{9,10},{10,1... | collective-permute-start | bytes 49160 | tf_op jit(solution)/shard_map/ppermute | solution.py:15
  217.1 1.9 collective-permute-start.27
  219.2 2.9 collective-permute-done.27
  224.2 2.8 collective-permute-start.29
  227.1 1.3 collective-permute-start.28
  229.1 2.7 collective-permute-done.28
  233.6 4.6 %collective-permute-start.30 = (bf16[1,1,32,256]{3,2,1,0:T(8,128)(2,1)S(1)}, bf16[1,1,32,256]{3,2,1,0:T(8,128)(2,1)S(1)}, u32[]{:S(2)}, u32[]{:S(2)}) collective-permute-start(bf16[1,1,32,256]{3,2,1,0:T(8,128)(2,1)S(1)} %get-tuple-element.23), channel_id=1, source_target_pairs={{0,1},{1,2},{2,3},{3,4},{4,5},{5,6},{6,7},{7,8},{8,9},{9,10},{10,1... | collective-permute-start | bytes 49160 | tf_op jit(solution)/shard_map/ppermute | solution.py:15
  238.1 1.9 collective-permute-start.31
  240.3 2.9 collective-permute-done.31
  245.3 3.0 collective-permute-start.33
  248.3 1.3 collective-permute-start.32
  250.5 2.5 collective-permute-done.32
  256.4 1.3 dynamic-slice
  257.7 81.4 %all-reduce.20.cloned.1.call-done = f32[8,12288]{1,0:T(8,128)} async-done(((f32[8,12288]{1,0:T(8,128)}), f32[8,12288]{1,0:T(8,128)}) %all-reduce.20.cloned.1.call-update) | async-done | bytes 393232
  339.1 2.3 dynamic-slice_bitcast_fusion
  341.4 8.0 %collective-permute-start.34 = (bf16[1,1,32,256]{3,2,1,0:T(8,128)(2,1)S(1)}, bf16[1,1,32,256]{3,2,1,0:T(8,128)(2,1)S(1)}, u32[]{:S(2)}, u32[]{:S(2)}) collective-permute-start(bf16[1,1,32,256]{3,2,1,0:T(8,128)(2,1)S(1)} %get-tuple-element.21), channel_id=1, source_target_pairs={{0,1},{1,2},{2,3},{3,4},{4,5},{5,6},{6,7},{7,8},{8,9},{9,10},{10,1... | collective-permute-start | bytes 49160 | tf_op jit(solution)/shard_map/ppermute | solution.py:15
  349.5 1.9 collective-permute-start.35
  351.4 3.1 collective-permute-done.35
  357.0 72.8 %all-gather.4.cloned.1.call-done = f32[64,1,12288]{2,1,0:T(1,128)} async-done(((f32[1,1,12288]{2,1,0:T(1,128)}), f32[64,1,12288]{2,1,0:T(1,128)}) %all-gather.4.cloned.1.call-update) | async-done | bytes 3145744 | tf_op jit(solution)/shard_map/all_gather | solution.py:157
  429.8 4.5 %reduce.2 = f32[12288]{0:T(1024)S(1)} reduce(f32[64,1,12288]{2,1,0:T(1,128)} %all-gather.4.cloned.1.call-done, f32[]{:T(128)} %constant.19.clone.1), dimensions={0,1}, to_apply=%region_2.3 | reduce | flops 774144 | bytes 3194884 | tf_op jit(solution)/shard_map/reduce_sum | solution.py:157
  (307 shorter events, 44.9 us)
Async XLA Ops:
  7.2 53.7 %all-to-all-start = ((bf16[1,8,2,32,256]{4,3,2,0,1:T(8,128)(2,1)}), bf16[1,8,2,32,256]{4,3,2,0,1:T(8,128)(2,1)S(1)}, u32[]{:S(2)}, u32[]{:S(2)}) async-start(bf16[1,8,2,32,256]{4,3,2,0,1:T(8,128)(2,1)} %bitcast.2014), calls=%async_computation | async-start | bytes 524288 | tf_op jit(solution)/shard_map/all_to_all | solution.py:127
  18.0 321.0 %all-reduce.20.cloned.1.call-start = ((), (), s32[]{:S(2)}) async-start(), calls=%async_computation.2 | async-start | bytes 786432
  60.9 16.5 %collective-permute-start = (bf16[8,1,1,32,256]{4,3,2,0,1:T(8,128)(2,1)S(1)}, bf16[8,1,1,32,256]{4,3,2,0,1:T(8,128)(2,1)S(1)}, u32[]{:S(2)}, u32[]{:S(2)}) collective-permute-start(bf16[8,1,1,32,256]{4,3,2,0,1:T(8,128)(2,1)S(1)} %get-tuple-element.19), channel_id=1, source_target_pairs={{0,1},{1,2},{2,3},{3,4},{4,5},{5,6},{6,7},{7,8},{8,9},{9,10},{10,1... | collective-permute-start | bytes 393224 | tf_op jit(solution)/shard_map/ppermute | solution.py:15
  75.4 6.3 %collective-permute-start.1 = (bf16[8,1,1,32,256]{4,3,2,0,1:T(8,128)(2,1)S(1)}, bf16[8,1,1,32,256]{4,3,2,0,1:T(8,128)(2,1)S(1)}, u32[]{:S(2)}, u32[]{:S(2)}) collective-permute-start(bf16[8,1,1,32,256]{4,3,2,0,1:T(8,128)(2,1)S(1)} %get-tuple-element.20), channel_id=1, source_target_pairs={{1,0},{2,1},{3,2},{4,3},{5,4},{6,5},{7,6},{8,7},{9,8},{10,9},{11,1... | collective-permute-start | bytes 393224 | tf_op jit(solution)/shard_map/ppermute | solution.py:18
  84.1 10.0 %copy-start = (bf16[1,2,32,256]{3,2,1,0:T(8,128)(2,1)S(1)}, bf16[1,2,32,256]{3,2,1,0:T(8,128)(2,1)}, u32[]{:S(2)}) copy-start(bf16[1,2,32,256]{3,2,1,0:T(8,128)(2,1)} %param.6) | copy-start | bytes 98308
  84.1 7.9 %collective-permute-start.3 = (bf16[8,1,2,32,256]{4,3,2,0,1:T(8,128)(2,1)S(1)}, bf16[8,1,2,32,256]{4,3,2,0,1:T(8,128)(2,1)S(1)}, u32[]{:S(2)}, u32[]{:S(2)}) collective-permute-start(bf16[8,1,2,32,256]{4,3,2,0,1:T(8,128)(2,1)S(1)} %bitcast.1997), channel_id=1, source_target_pairs={{64,0},{128,64},{192,128},{256,192},{320,256},{384,320},{448,384},... | collective-permute-start | bytes 786440 | tf_op jit(solution)/shard_map/ppermute | solution.py:18
  85.4 8.3 %collective-permute-start.2 = (bf16[8,1,2,32,256]{4,3,2,0,1:T(8,128)(2,1)S(1)}, bf16[8,1,2,32,256]{4,3,2,0,1:T(8,128)(2,1)S(1)}, u32[]{:S(2)}, u32[]{:S(2)}) collective-permute-start(bf16[8,1,2,32,256]{4,3,2,0,1:T(8,128)(2,1)S(1)} %bitcast.1998), channel_id=1, source_target_pairs={{0,64},{64,128},{128,192},{192,256},{256,320},{320,384},{384,448},... | collective-permute-start | bytes 786440 | tf_op jit(solution)/shard_map/ppermute | solution.py:15
  94.3 5.6 %collective-permute-start.5 = (bf16[1,2,32,256]{3,2,1,0:T(8,128)(2,1)S(1)}, bf16[1,2,32,256]{3,2,1,0:T(8,128)(2,1)S(1)}, u32[]{:S(2)}, u32[]{:S(2)}) collective-permute-start(bf16[1,2,32,256]{3,2,1,0:T(8,128)(2,1)S(1)} %fusion.86), channel_id=1, source_target_pairs={{0,64},{64,128},{128,192},{192,256},{256,320},{320,384},{384,448},... | collective-permute-start | bytes 98312 | tf_op jit(solution)/shard_map/ppermute | solution.py:15
  98.1 4.9 %collective-permute-start.4 = (bf16[1,2,32,256]{3,2,1,0:T(8,128)(2,1)S(1)}, bf16[1,2,32,256]{3,2,1,0:T(8,128)(2,1)S(1)}, u32[]{:S(2)}, u32[]{:S(2)}) collective-permute-start(bf16[1,2,32,256]{3,2,1,0:T(8,128)(2,1)S(1)} %fusion.86), channel_id=1, source_target_pairs={{64,0},{128,64},{192,128},{256,192},{320,256},{384,320},{448,384},... | collective-permute-start | bytes 98312 | tf_op jit(solution)/shard_map/ppermute | solution.py:18
  104.9 8.3 %collective-permute-start.6 = (bf16[1,1,32,256]{3,2,1,0:T(8,128)(2,1)S(1)}, bf16[1,1,32,256]{3,2,1,0:T(8,128)(2,1)S(1)}, u32[]{:S(2)}, u32[]{:S(2)}) collective-permute-start(bf16[1,1,32,256]{3,2,1,0:T(8,128)(2,1)S(1)} %get-tuple-element.35), channel_id=1, source_target_pairs={{0,1},{1,2},{2,3},{3,4},{4,5},{5,6},{6,7},{7,8},{8,9},{9,10},{10,1... | collective-permute-start | bytes 49160 | tf_op jit(solution)/shard_map/ppermute | solution.py:15
  111.1 5.1 %collective-permute-start.7 = (bf16[1,1,32,256]{3,2,1,0:T(8,128)(2,1)S(1)}, bf16[1,1,32,256]{3,2,1,0:T(8,128)(2,1)S(1)}, u32[]{:S(2)}, u32[]{:S(2)}) collective-permute-start(bf16[1,1,32,256]{3,2,1,0:T(8,128)(2,1)S(1)} %get-tuple-element.36), channel_id=1, source_target_pairs={{1,0},{2,1},{3,2},{4,3},{5,4},{6,5},{7,6},{8,7},{9,8},{10,9},{11,1... | collective-permute-start | bytes 49160 | tf_op jit(solution)/shard_map/ppermute | solution.py:18
  118.2 5.4 %collective-permute-start.9 = (bf16[1,2,32,256]{3,2,1,0:T(8,128)(2,1)S(1)}, bf16[1,2,32,256]{3,2,1,0:T(8,128)(2,1)S(1)}, u32[]{:S(2)}, u32[]{:S(2)}) collective-permute-start(bf16[1,2,32,256]{3,2,1,0:T(8,128)(2,1)S(1)} %get-tuple-element.37), channel_id=1, source_target_pairs={{0,64},{64,128},{128,192},{192,256},{256,320},{320,384},{384,448},... | collective-permute-start | bytes 98312 | tf_op jit(solution)/shard_map/ppermute | solution.py:15
  121.9 6.6 %collective-permute-start.8 = (bf16[1,2,32,256]{3,2,1,0:T(8,128)(2,1)S(1)}, bf16[1,2,32,256]{3,2,1,0:T(8,128)(2,1)S(1)}, u32[]{:S(2)}, u32[]{:S(2)}) collective-permute-start(bf16[1,2,32,256]{3,2,1,0:T(8,128)(2,1)S(1)} %get-tuple-element.37), channel_id=1, source_target_pairs={{64,0},{128,64},{192,128},{256,192},{320,256},{384,320},{448,384},... | collective-permute-start | bytes 98312 | tf_op jit(solution)/shard_map/ppermute | solution.py:18
  130.3 5.2 %collective-permute-start.10 = (bf16[1,1,32,256]{3,2,1,0:T(8,128)(2,1)S(1)}, bf16[1,1,32,256]{3,2,1,0:T(8,128)(2,1)S(1)}, u32[]{:S(2)}, u32[]{:S(2)}) collective-permute-start(bf16[1,1,32,256]{3,2,1,0:T(8,128)(2,1)S(1)} %get-tuple-element.33), channel_id=1, source_target_pairs={{0,1},{1,2},{2,3},{3,4},{4,5},{5,6},{6,7},{7,8},{8,9},{9,10},{10,1... | collective-permute-start | bytes 49160 | tf_op jit(solution)/shard_map/ppermute | solution.py:15
  133.4 5.1 %collective-permute-start.11 = (bf16[1,1,32,256]{3,2,1,0:T(8,128)(2,1)S(1)}, bf16[1,1,32,256]{3,2,1,0:T(8,128)(2,1)S(1)}, u32[]{:S(2)}, u32[]{:S(2)}) collective-permute-start(bf16[1,1,32,256]{3,2,1,0:T(8,128)(2,1)S(1)} %get-tuple-element.34), channel_id=1, source_target_pairs={{1,0},{2,1},{3,2},{4,3},{5,4},{6,5},{7,6},{8,7},{9,8},{10,9},{11,1... | collective-permute-start | bytes 49160 | tf_op jit(solution)/shard_map/ppermute | solution.py:18
  140.5 6.7 %collective-permute-start.13 = (bf16[1,2,32,256]{3,2,1,0:T(8,128)(2,1)S(1)}, bf16[1,2,32,256]{3,2,1,0:T(8,128)(2,1)S(1)}, u32[]{:S(2)}, u32[]{:S(2)}) collective-permute-start(bf16[1,2,32,256]{3,2,1,0:T(8,128)(2,1)S(1)} %get-tuple-element.39), channel_id=1, source_target_pairs={{0,64},{64,128},{128,192},{192,256},{256,320},{320,384},{384,448},... | collective-permute-start | bytes 98312 | tf_op jit(solution)/shard_map/ppermute | solution.py:15
  145.4 4.9 %collective-permute-start.12 = (bf16[1,2,32,256]{3,2,1,0:T(8,128)(2,1)S(1)}, bf16[1,2,32,256]{3,2,1,0:T(8,128)(2,1)S(1)}, u32[]{:S(2)}, u32[]{:S(2)}) collective-permute-start(bf16[1,2,32,256]{3,2,1,0:T(8,128)(2,1)S(1)} %get-tuple-element.39), channel_id=1, source_target_pairs={{64,0},{128,64},{192,128},{256,192},{320,256},{384,320},{448,384},... | collective-permute-start | bytes 98312 | tf_op jit(solution)/shard_map/ppermute | solution.py:18
  152.2 5.2 %collective-permute-start.14 = (bf16[1,1,32,256]{3,2,1,0:T(8,128)(2,1)S(1)}, bf16[1,1,32,256]{3,2,1,0:T(8,128)(2,1)S(1)}, u32[]{:S(2)}, u32[]{:S(2)}) collective-permute-start(bf16[1,1,32,256]{3,2,1,0:T(8,128)(2,1)S(1)} %get-tuple-element.31), channel_id=1, source_target_pairs={{0,1},{1,2},{2,3},{3,4},{4,5},{5,6},{6,7},{7,8},{8,9},{9,10},{10,1... | collective-permute-start | bytes 49160 | tf_op jit(solution)/shard_map/ppermute | solution.py:15
  155.3 5.1 %collective-permute-start.15 = (bf16[1,1,32,256]{3,2,1,0:T(8,128)(2,1)S(1)}, bf16[1,1,32,256]{3,2,1,0:T(8,128)(2,1)S(1)}, u32[]{:S(2)}, u32[]{:S(2)}) collective-permute-start(bf16[1,1,32,256]{3,2,1,0:T(8,128)(2,1)S(1)} %get-tuple-element.32), channel_id=1, source_target_pairs={{1,0},{2,1},{3,2},{4,3},{5,4},{6,5},{7,6},{8,7},{9,8},{10,9},{11,1... | collective-permute-start | bytes 49160 | tf_op jit(solution)/shard_map/ppermute | solution.py:18
  162.4 5.4 %collective-permute-start.17 = (bf16[1,2,32,256]{3,2,1,0:T(8,128)(2,1)S(1)}, bf16[1,2,32,256]{3,2,1,0:T(8,128)(2,1)S(1)}, u32[]{:S(2)}, u32[]{:S(2)}) collective-permute-start(bf16[1,2,32,256]{3,2,1,0:T(8,128)(2,1)S(1)} %get-tuple-element.41), channel_id=1, source_target_pairs={{0,64},{64,128},{128,192},{192,256},{256,320},{320,384},{384,448},... | collective-permute-start | bytes 98312 | tf_op jit(solution)/shard_map/ppermute | solution.py:15
  166.1 4.7 %collective-permute-start.16 = (bf16[1,2,32,256]{3,2,1,0:T(8,128)(2,1)S(1)}, bf16[1,2,32,256]{3,2,1,0:T(8,128)(2,1)S(1)}, u32[]{:S(2)}, u32[]{:S(2)}) collective-permute-start(bf16[1,2,32,256]{3,2,1,0:T(8,128)(2,1)S(1)} %get-tuple-element.41), channel_id=1, source_target_pairs={{64,0},{128,64},{192,128},{256,192},{320,256},{384,320},{448,384},... | collective-permute-start | bytes 98312 | tf_op jit(solution)/shard_map/ppermute | solution.py:18
  172.6 5.5 %collective-permute-start.18 = (bf16[1,1,32,256]{3,2,1,0:T(8,128)(2,1)S(1)}, bf16[1,1,32,256]{3,2,1,0:T(8,128)(2,1)S(1)}, u32[]{:S(2)}, u32[]{:S(2)}) collective-permute-start(bf16[1,1,32,256]{3,2,1,0:T(8,128)(2,1)S(1)} %get-tuple-element.29), channel_id=1, source_target_pairs={{0,1},{1,2},{2,3},{3,4},{4,5},{5,6},{6,7},{7,8},{8,9},{9,10},{10,1... | collective-permute-start | bytes 49160 | tf_op jit(solution)/shard_map/ppermute | solution.py:15
  175.9 5.1 %collective-permute-start.19 = (bf16[1,1,32,256]{3,2,1,0:T(8,128)(2,1)S(1)}, bf16[1,1,32,256]{3,2,1,0:T(8,128)(2,1)S(1)}, u32[]{:S(2)}, u32[]{:S(2)}) collective-permute-start(bf16[1,1,32,256]{3,2,1,0:T(8,128)(2,1)S(1)} %get-tuple-element.30), channel_id=1, source_target_pairs={{1,0},{2,1},{3,2},{4,3},{5,4},{6,5},{7,6},{8,7},{9,8},{10,9},{11,1... | collective-permute-start | bytes 49160 | tf_op jit(solution)/shard_map/ppermute | solution.py:18
  183.1 4.7 %collective-permute-start.21 = (bf16[1,2,32,256]{3,2,1,0:T(8,128)(2,1)S(1)}, bf16[1,2,32,256]{3,2,1,0:T(8,128)(2,1)S(1)}, u32[]{:S(2)}, u32[]{:S(2)}) collective-permute-start(bf16[1,2,32,256]{3,2,1,0:T(8,128)(2,1)S(1)} %get-tuple-element.43), channel_id=1, source_target_pairs={{0,64},{64,128},{128,192},{192,256},{256,320},{320,384},{384,448},... | collective-permute-start | bytes 98312 | tf_op jit(solution)/shard_map/ppermute | solution.py:15
  185.9 4.7 %collective-permute-start.20 = (bf16[1,2,32,256]{3,2,1,0:T(8,128)(2,1)S(1)}, bf16[1,2,32,256]{3,2,1,0:T(8,128)(2,1)S(1)}, u32[]{:S(2)}, u32[]{:S(2)}) collective-permute-start(bf16[1,2,32,256]{3,2,1,0:T(8,128)(2,1)S(1)} %get-tuple-element.43), channel_id=1, source_target_pairs={{64,0},{128,64},{192,128},{256,192},{320,256},{384,320},{448,384},... | collective-permute-start | bytes 98312 | tf_op jit(solution)/shard_map/ppermute | solution.py:18
  192.4 5.6 %collective-permute-start.22 = (bf16[1,1,32,256]{3,2,1,0:T(8,128)(2,1)S(1)}, bf16[1,1,32,256]{3,2,1,0:T(8,128)(2,1)S(1)}, u32[]{:S(2)}, u32[]{:S(2)}) collective-permute-start(bf16[1,1,32,256]{3,2,1,0:T(8,128)(2,1)S(1)} %get-tuple-element.27), channel_id=1, source_target_pairs={{0,1},{1,2},{2,3},{3,4},{4,5},{5,6},{6,7},{7,8},{8,9},{9,10},{10,1... | collective-permute-start | bytes 49160 | tf_op jit(solution)/shard_map/ppermute | solution.py:15
  196.0 5.1 %collective-permute-start.23 = (bf16[1,1,32,256]{3,2,1,0:T(8,128)(2,1)S(1)}, bf16[1,1,32,256]{3,2,1,0:T(8,128)(2,1)S(1)}, u32[]{:S(2)}, u32[]{:S(2)}) collective-permute-start(bf16[1,1,32,256]{3,2,1,0:T(8,128)(2,1)S(1)} %get-tuple-element.28), channel_id=1, source_target_pairs={{1,0},{2,1},{3,2},{4,3},{5,4},{6,5},{7,6},{8,7},{9,8},{10,9},{11,1... | collective-permute-start | bytes 49160 | tf_op jit(solution)/shard_map/ppermute | solution.py:18
  203.1 4.7 %collective-permute-start.25 = (bf16[1,2,32,256]{3,2,1,0:T(8,128)(2,1)S(1)}, bf16[1,2,32,256]{3,2,1,0:T(8,128)(2,1)S(1)}, u32[]{:S(2)}, u32[]{:S(2)}) collective-permute-start(bf16[1,2,32,256]{3,2,1,0:T(8,128)(2,1)S(1)} %get-tuple-element.45), channel_id=1, source_target_pairs={{0,64},{64,128},{128,192},{192,256},{256,320},{320,384},{384,448},... | collective-permute-start | bytes 98312 | tf_op jit(solution)/shard_map/ppermute | solution.py:15
  206.0 4.7 %collective-permute-start.24 = (bf16[1,2,32,256]{3,2,1,0:T(8,128)(2,1)S(1)}, bf16[1,2,32,256]{3,2,1,0:T(8,128)(2,1)S(1)}, u32[]{:S(2)}, u32[]{:S(2)}) collective-permute-start(bf16[1,2,32,256]{3,2,1,0:T(8,128)(2,1)S(1)} %get-tuple-element.45), channel_id=1, source_target_pairs={{64,0},{128,64},{192,128},{256,192},{320,256},{384,320},{448,384},... | collective-permute-start | bytes 98312 | tf_op jit(solution)/shard_map/ppermute | solution.py:18
  212.5 6.7 %collective-permute-start.26 = (bf16[1,1,32,256]{3,2,1,0:T(8,128)(2,1)S(1)}, bf16[1,1,32,256]{3,2,1,0:T(8,128)(2,1)S(1)}, u32[]{:S(2)}, u32[]{:S(2)}) collective-permute-start(bf16[1,1,32,256]{3,2,1,0:T(8,128)(2,1)S(1)} %get-tuple-element.25), channel_id=1, source_target_pairs={{0,1},{1,2},{2,3},{3,4},{4,5},{5,6},{6,7},{7,8},{8,9},{9,10},{10,1... | collective-permute-start | bytes 49160 | tf_op jit(solution)/shard_map/ppermute | solution.py:15
  217.1 5.1 %collective-permute-start.27 = (bf16[1,1,32,256]{3,2,1,0:T(8,128)(2,1)S(1)}, bf16[1,1,32,256]{3,2,1,0:T(8,128)(2,1)S(1)}, u32[]{:S(2)}, u32[]{:S(2)}) collective-permute-start(bf16[1,1,32,256]{3,2,1,0:T(8,128)(2,1)S(1)} %get-tuple-element.26), channel_id=1, source_target_pairs={{1,0},{2,1},{3,2},{4,3},{5,4},{6,5},{7,6},{8,7},{9,8},{10,9},{11,1... | collective-permute-start | bytes 49160 | tf_op jit(solution)/shard_map/ppermute | solution.py:18
  224.2 4.7 %collective-permute-start.29 = (bf16[1,2,32,256]{3,2,1,0:T(8,128)(2,1)S(1)}, bf16[1,2,32,256]{3,2,1,0:T(8,128)(2,1)S(1)}, u32[]{:S(2)}, u32[]{:S(2)}) collective-permute-start(bf16[1,2,32,256]{3,2,1,0:T(8,128)(2,1)S(1)} %get-tuple-element.47), channel_id=1, source_target_pairs={{0,64},{64,128},{128,192},{192,256},{256,320},{320,384},{384,448},... | collective-permute-start | bytes 98312 | tf_op jit(solution)/shard_map/ppermute | solution.py:15
  227.1 4.7 %collective-permute-start.28 = (bf16[1,2,32,256]{3,2,1,0:T(8,128)(2,1)S(1)}, bf16[1,2,32,256]{3,2,1,0:T(8,128)(2,1)S(1)}, u32[]{:S(2)}, u32[]{:S(2)}) collective-permute-start(bf16[1,2,32,256]{3,2,1,0:T(8,128)(2,1)S(1)} %get-tuple-element.47), channel_id=1, source_target_pairs={{64,0},{128,64},{192,128},{256,192},{320,256},{384,320},{448,384},... | collective-permute-start | bytes 98312 | tf_op jit(solution)/shard_map/ppermute | solution.py:18
  233.6 6.7 %collective-permute-start.30 = (bf16[1,1,32,256]{3,2,1,0:T(8,128)(2,1)S(1)}, bf16[1,1,32,256]{3,2,1,0:T(8,128)(2,1)S(1)}, u32[]{:S(2)}, u32[]{:S(2)}) collective-permute-start(bf16[1,1,32,256]{3,2,1,0:T(8,128)(2,1)S(1)} %get-tuple-element.23), channel_id=1, source_target_pairs={{0,1},{1,2},{2,3},{3,4},{4,5},{5,6},{6,7},{7,8},{8,9},{9,10},{10,1... | collective-permute-start | bytes 49160 | tf_op jit(solution)/shard_map/ppermute | solution.py:15
  238.1 5.1 %collective-permute-start.31 = (bf16[1,1,32,256]{3,2,1,0:T(8,128)(2,1)S(1)}, bf16[1,1,32,256]{3,2,1,0:T(8,128)(2,1)S(1)}, u32[]{:S(2)}, u32[]{:S(2)}) collective-permute-start(bf16[1,1,32,256]{3,2,1,0:T(8,128)(2,1)S(1)} %get-tuple-element.24), channel_id=1, source_target_pairs={{1,0},{2,1},{3,2},{4,3},{5,4},{6,5},{7,6},{8,7},{9,8},{10,9},{11,1... | collective-permute-start | bytes 49160 | tf_op jit(solution)/shard_map/ppermute | solution.py:18
  245.3 5.0 %collective-permute-start.33 = (bf16[1,2,32,256]{3,2,1,0:T(8,128)(2,1)S(1)}, bf16[1,2,32,256]{3,2,1,0:T(8,128)(2,1)S(1)}, u32[]{:S(2)}, u32[]{:S(2)}) collective-permute-start(bf16[1,2,32,256]{3,2,1,0:T(8,128)(2,1)S(1)} %get-tuple-element.49), channel_id=1, source_target_pairs={{0,64},{64,128},{128,192},{192,256},{256,320},{320,384},{384,448},... | collective-permute-start | bytes 98312 | tf_op jit(solution)/shard_map/ppermute | solution.py:15
  248.3 4.7 %collective-permute-start.32 = (bf16[1,2,32,256]{3,2,1,0:T(8,128)(2,1)S(1)}, bf16[1,2,32,256]{3,2,1,0:T(8,128)(2,1)S(1)}, u32[]{:S(2)}, u32[]{:S(2)}) collective-permute-start(bf16[1,2,32,256]{3,2,1,0:T(8,128)(2,1)S(1)} %get-tuple-element.49), channel_id=1, source_target_pairs={{64,0},{128,64},{192,128},{256,192},{320,256},{384,320},{448,384},... | collective-permute-start | bytes 98312 | tf_op jit(solution)/shard_map/ppermute | solution.py:18
  256.3 173.4 %all-gather.4.cloned.1.call-start = ((), (), s32[]{:S(2)}) async-start(), calls=%async_computation.1 | async-start | bytes 3194880 | tf_op jit(solution)/shard_map/all_gather | solution.py:157
  341.4 10.0 %collective-permute-start.34 = (bf16[1,1,32,256]{3,2,1,0:T(8,128)(2,1)S(1)}, bf16[1,1,32,256]{3,2,1,0:T(8,128)(2,1)S(1)}, u32[]{:S(2)}, u32[]{:S(2)}) collective-permute-start(bf16[1,1,32,256]{3,2,1,0:T(8,128)(2,1)S(1)} %get-tuple-element.21), channel_id=1, source_target_pairs={{0,1},{1,2},{2,3},{3,4},{4,5},{5,6},{6,7},{7,8},{8,9},{9,10},{10,1... | collective-permute-start | bytes 49160 | tf_op jit(solution)/shard_map/ppermute | solution.py:15
  349.5 5.1 %collective-permute-start.35 = (bf16[1,1,32,256]{3,2,1,0:T(8,128)(2,1)S(1)}, bf16[1,1,32,256]{3,2,1,0:T(8,128)(2,1)S(1)}, u32[]{:S(2)}, u32[]{:S(2)}) collective-permute-start(bf16[1,1,32,256]{3,2,1,0:T(8,128)(2,1)S(1)} %get-tuple-element.22), channel_id=1, source_target_pairs={{1,0},{2,1},{3,2},{4,3},{5,4},{6,5},{7,6},{8,7},{9,8},{10,9},{11,1... | collective-permute-start | bytes 49160 | tf_op jit(solution)/shard_map/ppermute | solution.py:18
Sparse Core Ops, SparseCore 0:
  256.5 82.5 all-reduce.19
  343.5 86.2 all-gather.3
